TPU v7x, 32 devices: a whole 2x2x4 slice. The times are simulated.
32 devices in a mesh: rows: 4 (over y, x), cols: 8 (over z, core).
Axes of the slice: x: 2, y: 2, z: 4, core: 2. Of those that a mesh axis runs over, the one named last changes fastest.
Arguments:
- features: bfloat16 [32, 128, 1024], P('rows', 'cols'), may hold values from -24 to 24
- w_query: bfloat16 [1024, 1024], replicated, may hold values from -0.1875 to 0.1875
- w_key: bfloat16 [1024, 1024], replicated, may hold values from -0.1875 to 0.1875
- w_value: bfloat16 [1024, 1024], replicated, may hold values from -0.1875 to 0.1875
- w_out: bfloat16 [1024, 1024], replicated, may hold values from -0.1875 to 0.1875
- reg_pos: int32 [32], replicated, may hold values from 0 to 4095, as said below
- grad_out: bfloat16 [32, 128, 1024], P('rows', 'cols'), may hold values from -6 to 6
Outputs:
- layer_out: bfloat16 [32, 128, 1024], P('rows', 'cols')
- grad_in: bfloat16 [32, 128, 1024], P('rows', 'cols')
Inputs may be any that keep to these rules, and one draw needn't show every extreme that they name: The 32 global tokens are distinct, one in each tile of 128 tokens: reg_pos[r] lies in tile row r // 8 and tile column r % 8, tiles counted row by row.
All inputs are finite; a program needn't handle non-finite values.
Results may differ from a plain program's by a relative error of at most 0.03.
The roundings to bfloat16 on the way count: a program that leaves them out, or rounds other values in their place, can miss the bound.
Values may be sent and summed in bfloat16 or wider, within the bound.
No kernel may reach another device: no remote copies, remote signals or barrier semaphores. Data moves between devices by JAX's collectives and lax.ppermute only.
A program may use at most 128 MiB of HBM per device.

v0:
```python
import math
import jax
import jax.numpy as jnp
from jax import lax
from jax.sharding import PartitionSpec as P

HEADS = 16
KW = 13
RAD = 6


def with_halo(block, sides, width):
    for axis, dim in sides:
        count = lax.axis_size(axis)
        forward = [(i, i + 1) for i in range(count - 1)]
        backward = [(target, source) for source, target in forward]
        low = lax.ppermute(
            lax.slice_in_dim(block, block.shape[dim] - width, None, axis=dim), axis, forward
        )
        high = lax.ppermute(lax.slice_in_dim(block, 0, width, axis=dim), axis, backward)
        block = jnp.concatenate([low, block, high], axis=dim)
    return block


def from_behind(x, axis, by):
    size = lax.axis_size(axis)
    pairs = [(i, i + by) for i in range(size) if 0 <= i + by < size]
    return lax.ppermute(x, axis, pairs)


def axis_valid(first_cell, tile, extent):
    query_cell = first_cell + jnp.arange(tile, dtype=jnp.int32)[:, None]
    key_cell = first_cell - RAD + jnp.arange(tile + 2 * RAD, dtype=jnp.int32)[None, :]
    window_start = jnp.clip(query_cell - RAD, 0, extent - KW)
    return (key_cell >= window_start) & (key_cell <= window_start + KW - 1)


def einsum_wide(form, left, right):
    return jnp.einsum(form, left, right, preferred_element_type=jnp.float32)


def to_heads(x):
    count, width = x.shape
    return x.reshape(count, HEADS, width // HEADS).transpose(1, 0, 2)


def from_heads(x):
    heads, count, size = x.shape
    return x.transpose(1, 0, 2).reshape(count, heads * size)


def shards(features, w_query, w_key, w_value, w_out, reg_pos, grad_out):
    tile_rows, tile_cols, model_width = features.shape
    head_size = model_width // HEADS
    score_scale = 1.0 / math.sqrt(head_size)
    row_count = lax.axis_size("rows")
    col_count = lax.axis_size("cols")
    row_index = lax.axis_index("rows")
    col_index = lax.axis_index("cols")
    band_cols = tile_cols * col_count
    first_row = row_index * tile_rows
    first_col = col_index * tile_cols
    tokens = tile_rows * tile_cols
    frame_rows = tile_rows + 2 * RAD
    frame_cols = tile_cols + 2 * RAD
    flat_tokens = features.reshape(-1, model_width)
    queries = jnp.dot(flat_tokens, w_query, preferred_element_type=jnp.float32).astype(jnp.bfloat16)
    keys_local = jnp.dot(flat_tokens, w_key, preferred_element_type=jnp.float32).astype(
        jnp.bfloat16
    )
    values_local = jnp.dot(flat_tokens, w_value, preferred_element_type=jnp.float32).astype(
        jnp.bfloat16
    )
    key_value = jnp.concatenate([keys_local, values_local], axis=1)
    own_index = row_index * col_count + col_index
    own_place = lax.dynamic_index_in_dim(reg_pos, own_index, 0, keepdims=False)
    own_local = (own_place // band_cols - first_row) * tile_cols + (
        own_place % band_cols - first_col
    )
    own_kv = lax.dynamic_slice_in_dim(key_value, own_local, 1, 0)
    global_kv = lax.all_gather(own_kv, ("rows", "cols"), axis=0, tiled=True)
    framed = with_halo(
        key_value.reshape(tile_rows, tile_cols, 2 * model_width), (("rows", 0), ("cols", 1)), RAD
    ).reshape(frame_rows * frame_cols, 2 * model_width)
    all_kv = jnp.concatenate([framed, global_kv], axis=0)
    key_count = all_kv.shape[0]
    row_valid = axis_valid(first_row, tile_rows, tile_rows * row_count)
    col_valid = axis_valid(first_col, tile_cols, band_cols)
    window_mask = (row_valid[:, None, :, None] & col_valid[None, :, None, :]).reshape(
        tokens, frame_rows * frame_cols
    )
    full_mask = jnp.concatenate(
        [window_mask, jnp.ones((tokens, key_count - frame_rows * frame_cols), jnp.bool_)], axis=1
    )
    query_heads = to_heads(queries)
    key_heads = to_heads(all_kv[:, :model_width])
    value_heads = to_heads(all_kv[:, model_width:])
    scores = einsum_wide("hqd,hkd->hqk", query_heads, key_heads) * score_scale
    scores = jnp.where(full_mask[None], scores, -1e30)
    row_max = jnp.max(scores, axis=-1, keepdims=True)
    exps = jnp.exp(scores - row_max)
    denominator = jnp.sum(exps, axis=-1, keepdims=True)
    probs = exps / denominator
    rounded = probs.astype(jnp.bfloat16)
    attended_heads = einsum_wide("hqk,hkd->hqd", rounded, value_heads).astype(jnp.bfloat16)
    attended = from_heads(attended_heads)
    layer_out = (
        jnp.dot(attended, w_out, preferred_element_type=jnp.float32)
        .astype(jnp.bfloat16)
        .reshape(features.shape)
    )
    grad_attended = jnp.dot(
        grad_out.reshape(-1, model_width), w_out.T, preferred_element_type=jnp.float32
    ).astype(jnp.bfloat16)
    grad_heads = to_heads(grad_attended)
    delta = einsum_wide("hqd,hqd->hq", grad_heads, attended_heads)[..., None]
    dots = einsum_wide("hqd,hkd->hqk", grad_heads, value_heads)
    slopes = (probs * (dots - delta) * score_scale).astype(jnp.bfloat16)
    query_grads = from_heads(einsum_wide("hqk,hkd->hqd", slopes, key_heads).astype(jnp.bfloat16))
    key_grads = from_heads(einsum_wide("hqk,hqd->hkd", slopes, query_heads))
    value_grads = from_heads(einsum_wide("hqk,hqd->hkd", rounded, grad_heads))
    kv_grads_all = jnp.concatenate([key_grads, value_grads], axis=1)
    global_grads = kv_grads_all[frame_rows * frame_cols :]
    own_grads = lax.psum_scatter(global_grads, ("rows", "cols"), scatter_dimension=0, tiled=True)
    frame_grads = kv_grads_all[: frame_rows * frame_cols].reshape(
        frame_rows, frame_cols, 2 * model_width
    )
    left_rim = frame_grads[:, :RAD]
    right_rim = frame_grads[:, tile_cols + RAD :]
    centre = frame_grads[:, RAD : tile_cols + RAD]
    from_right = from_behind(left_rim.astype(jnp.bfloat16), "cols", -1).astype(left_rim.dtype)
    from_left = from_behind(right_rim.astype(jnp.bfloat16), "cols", 1).astype(right_rim.dtype)
    centre = centre.at[:, tile_cols - RAD :].add(from_right).at[:, :RAD].add(from_left)
    upper_rim = centre[:RAD]
    lower_rim = centre[tile_rows + RAD :]
    middle = centre[RAD : tile_rows + RAD]
    from_below = from_behind(upper_rim.astype(jnp.bfloat16), "rows", -1).astype(upper_rim.dtype)
    from_above = from_behind(lower_rim.astype(jnp.bfloat16), "rows", 1).astype(lower_rim.dtype)
    middle = middle.at[tile_rows - RAD :].add(from_below).at[:RAD].add(from_above)
    middle = middle.reshape(tokens, 2 * model_width)
    own_row = lax.dynamic_slice_in_dim(middle, own_local, 1, 0) + own_grads
    kv_grads = lax.dynamic_update_slice_in_dim(middle, own_row, own_local, 0).astype(jnp.bfloat16)
    grad_in = (
        jnp.dot(query_grads, w_query.T, preferred_element_type=jnp.float32)
        + jnp.dot(kv_grads[:, :model_width], w_key.T, preferred_element_type=jnp.float32)
        + jnp.dot(kv_grads[:, model_width:], w_value.T, preferred_element_type=jnp.float32)
    )
    grad_in = grad_in.astype(jnp.bfloat16).reshape(features.shape)
    return (layer_out, grad_in)


def solution(mesh):
    placed = (P("rows", "cols", None), P(), P(), P(), P(), P(), P("rows", "cols", None))
    return jax.shard_map(
        shards,
        mesh=mesh,
        in_specs=placed,
        out_specs=(P("rows", "cols", None), P("rows", "cols", None)),
        check_vma=False,
    )
```

profile of v0, /device:TPU:0, one launch (start us, length us, event | category | flops | bytes accessed | tf_op | source)
XLA Modules:
  0.0 321.7 jit_solution(17571939604907091626)
XLA Ops:
  7.2 2.3 convolution_convert_fusion.4
  11.3 5.6 %collective-permute-start = (bf16[6,16,2048]{2,0,1:T(8,128)(2,1)}, bf16[6,16,2048]{2,0,1:T(8,128)(2,1)}, u32[]{:S(2)}, u32[]{:S(2)}) collective-permute-start(bf16[6,16,2048]{2,0,1:T(8,128)(2,1)} %copy.41), channel_id=1, source_target_pairs={{0,8},{8,16},{16,24},{1,9},{9,17},{17,25},{2,10},{10,18},{18,26},{... | collective-permute-start | bytes 1179656 | tf_op jit(solution)/shard_map/ppermute | solution.py:17
  22.6 2.8 convolution_convert_fusion.6
  27.6 13.2 %collective-permute-done.1 = bf16[6,16,2048]{2,0,1:T(8,128)(2,1)} collective-permute-done((bf16[6,16,2048]{2,0,1:T(8,128)(2,1)}, bf16[6,16,2048]{2,0,1:T(8,128)(2,1)}, u32[]{:S(2)}, u32[]{:S(2)}) %collective-permute-start.1) | collective-permute-done | bytes 393248 | tf_op jit(solution)/shard_map/ppermute | solution.py:20
  40.8 2.7 pad_maximum_fusion.5
  43.5 2.1 collective-permute-start.2
  46.9 43.1 %all-gather = bf16[32,1,2048]{2,1,0:T(2,128)(2,1)S(1)} all-gather(bf16[1,1,2048]{2,1,0:T(2,128)(2,1)S(1)} %fusion.19), channel_id=1, replica_groups=mesh['rows'=4,'cols'=8] {'rows','cols'}, dimensions={0}, use_global_device_ids=true | all-gather | bytes 135168 | tf_op jit(solution)/shard_map/all_gather | solution.py:81
  92.8 2.4 pad_maximum_fusion
  95.2 2.8 copy.44
  98.0 4.0 %reshape.324 = bf16[560,2048]{1,0:T(8,128)(2,1)} reshape(bf16[20,28,2048]{2,1,0:T(8,128)(2,1)} %copy.44) | data formatting | bytes 4587520 | tf_op jit(solution)/shard_map/reshape | solution.py:84
  102.0 3.3 %pad_maximum_fusion.1 = (bf16[592,1024]{1,0:T(8,128)(2,1)}, bf16[592,1024]{1,0:T(8,128)(2,1)}) fusion(bf16[32,2048]{1,0:T(8,128)(2,1)S(1)} %bitcast.90, bf16[560,2048]{1,0:T(8,128)(2,1)} %reshape.324), kind=kLoop, calls=%fused_computation.21 | loop fusion | flops 4849664 | bytes 4849664 | tf_op jit(solution)/shard_map/concatenate | solution.py:85
  106.9 2.4 copy.46
  109.4 5.0 %fusion.24 = (f32[16,128]{1,0:T(8,128)S(1)}, f32[16,128,592]{1,2,0:T(8,128)}) fusion(pred[128,592]{0,1:T(8,128)(4,1)S(1)} %concatenate.26.clone, bf16[16,128,64]{1,2,0:T(8,128)(2,1)} %bitcast.87, bf16[16,592,64]{1,2,0:T(8,128)(2,1)S(1)} %bitcast.72), kind=kOutput, calls=%fused_computation.69 | convolution fusion | flops 160039504 | bytes 6408192 | tf_op jit(solution)/shard_map/sub | solution.py:101
  114.4 2.9 fusion.6
  118.6 2.4 fusion.27
  122.4 2.4 fusion.26
  124.9 3.2 copy.49
  128.1 3.2 copy.48
  131.3 5.0 %fusion.1 = f32[560,2048]{1,0:T(8,128)} fusion(f32[592,1024]{1,0:T(8,128)} %copy.48, f32[592,1024]{1,0:T(8,128)} %copy.49), kind=kLoop, calls=%fused_computation.6 | loop fusion | flops 1146880 | bytes 9437184 | tf_op jit(solution)/shard_map/concatenate | solution.py:122
  136.3 5.4 %reshape.334 = f32[20,28,2048]{2,1,0:T(8,128)} reshape(f32[560,2048]{1,0:T(8,128)} %fusion.1) | data formatting | bytes 9175040 | tf_op jit(solution)/shard_map/reshape | solution.py:125
  141.7 3.0 convert.8
  145.8 2.0 slice.186
  150.7 3.9 %collective-permute-start.5 = (bf16[20,6,2048]{2,0,1:T(8,128)(2,1)}, bf16[20,6,2048]{2,0,1:T(8,128)(2,1)}, u32[]{:S(2)}, u32[]{:S(2)}) collective-permute-start(bf16[20,6,2048]{2,0,1:T(8,128)(2,1)} %copy.52), channel_id=1, source_target_pairs={{0,1},{1,2},{2,3},{3,4},{4,5},{5,6},{6,7},{8,9},{9,10},{10,11},{11... | collective-permute-start | bytes 1474568 | tf_op jit(solution)/shard_map/ppermute | solution.py:28
  157.5 6.2 %scatter-add.14 = f32[20,16,2048]{2,1,0:T(8,128)} dynamic-update-slice(f32[20,16,2048]{2,1,0:T(8,128)} %slice.186, f32[20,6,2048]{2,1,0:T(8,128)S(1)} %slice_add_fusion.1, s32[]{:T(128)} %constant.163.clone.1, s32[]{:T(128)} %constant.180.clone.1, s32[]{:T(128)} %constant.163.clone.1) | dynamic-update-slice | bytes 1966084 | tf_op jit(solution)/shard_map/scatter-add | solution.py:133
  163.7 1.8 slice_add_fusion
  165.5 7.0 %scatter-add.15 = f32[20,16,2048]{2,1,0:T(8,128)} dynamic-update-slice(f32[20,16,2048]{2,1,0:T(8,128)} %scatter-add.14, f32[20,6,2048]{2,1,0:T(8,128)S(1)} %slice_add_fusion, s32[]{:T(128)} %constant.163.clone.1, s32[]{:T(128)} %constant.163.clone.1, s32[]{:T(128)} %constant.163.clone.1) | dynamic-update-slice | bytes 1966084 | tf_op jit(solution)/shard_map/scatter-add | solution.py:133
  172.5 2.1 convert.9
  177.6 3.4 %fusion.25 = f32[128,1024]{1,0:T(8,128)} fusion(bf16[128,1024]{0,1:T(8,128)(2,1)S(1)} %bitcast.89, bf16[1024,1024]{1,0:T(8,128)(2,1)} %param.16), kind=kOutput, calls=%fused_computation.70 | convolution fusion | flops 268435456 | bytes 2883584 | tf_op jit(solution)/shard_map/dot_general | solution.py:144
  181.1 4.6 %collective-permute-start.7 = (bf16[6,16,2048]{2,1,0:T(8,128)(2,1)S(1)}, bf16[6,16,2048]{2,1,0:T(8,128)(2,1)S(1)}, u32[]{:S(2)}, u32[]{:S(2)}) collective-permute-start(bf16[6,16,2048]{2,1,0:T(8,128)(2,1)S(1)} %get-tuple-element.56), channel_id=1, source_target_pairs={{0,8},{8,16},{16,24},{1,9},{9,17},{17,25},{2,10},{10,18},{18,26},{... | collective-permute-start | bytes 1179656 | tf_op jit(solution)/shard_map/ppermute | solution.py:28
  187.9 4.8 %collective-permute-done.7 = bf16[6,16,2048]{2,1,0:T(8,128)(2,1)S(1)} collective-permute-done((bf16[6,16,2048]{2,1,0:T(8,128)(2,1)S(1)}, bf16[6,16,2048]{2,1,0:T(8,128)(2,1)S(1)}, u32[]{:S(2)}, u32[]{:S(2)}) %collective-permute-start.7) | collective-permute-done | bytes 393248 | tf_op jit(solution)/shard_map/ppermute | solution.py:28
  192.9 116.6 %all-reduce.4.cloned.1.call-done = f32[32,2048]{1,0:T(8,128)} async-done(((f32[32,2048]{1,0:T(8,128)}), f32[32,2048]{1,0:T(8,128)}) %all-reduce.4.cloned.1.call-update) | async-done | bytes 262160
  310.7 2.6 convolution_add_fusion.1
  (93 shorter events, 30.4 us)
Async XLA Ops:
  7.2 18.6 %copy-start = (bf16[1024,1024]{1,0:T(8,128)(2,1)S(1)}, bf16[1024,1024]{1,0:T(8,128)(2,1)}, u32[]{:S(2)}) copy-start(bf16[1024,1024]{1,0:T(8,128)(2,1)} %param.19) | copy-start | bytes 6291460
  7.2 2.3 copy-start.10
  7.2 302.3 %all-reduce.4.cloned.1.call-start = ((), (), s32[]{:S(2)}) async-start(), calls=%async_computation | async-start | bytes 524288
  7.2 2.5 copy-start.8
  9.7 9.6 %copy-start.17 = (s32[32]{0:T(128)S(1)}, s32[32]{0:T(128)}, u32[]{:S(2)}) copy-start(s32[32]{0:T(128)} %param.20) | copy-start | bytes 388
  11.3 16.3 %collective-permute-start = (bf16[6,16,2048]{2,0,1:T(8,128)(2,1)}, bf16[6,16,2048]{2,0,1:T(8,128)(2,1)}, u32[]{:S(2)}, u32[]{:S(2)}) collective-permute-start(bf16[6,16,2048]{2,0,1:T(8,128)(2,1)} %copy.41), channel_id=1, source_target_pairs={{0,8},{8,16},{16,24},{1,9},{9,17},{17,25},{2,10},{10,18},{18,26},{... | collective-permute-start | bytes 1179656 | tf_op jit(solution)/shard_map/ppermute | solution.py:17
  18.0 22.8 %collective-permute-start.1 = (bf16[6,16,2048]{2,0,1:T(8,128)(2,1)}, bf16[6,16,2048]{2,0,1:T(8,128)(2,1)}, u32[]{:S(2)}, u32[]{:S(2)}) collective-permute-start(bf16[6,16,2048]{2,0,1:T(8,128)(2,1)} %copy.42), channel_id=1, source_target_pairs={{8,0},{16,8},{24,16},{9,1},{17,9},{25,17},{10,2},{18,10},{26,18},{... | collective-permute-start | bytes 1179656 | tf_op jit(solution)/shard_map/ppermute | solution.py:20
  22.6 3.2 copy-start.16
  25.8 64.2 %copy-start.13 = (bf16[128,1024]{1,0:T(8,128)(2,1)S(1)}, bf16[128,1024]{1,0:T(8,128)(2,1)}, u32[]{:S(2)}) copy-start(bf16[128,1024]{1,0:T(8,128)(2,1)} %convolution_convert_fusion.6) | copy-start | bytes 786436
  43.5 49.3 %collective-permute-start.2 = (bf16[20,6,2048]{2,0,1:T(8,128)(2,1)}, bf16[20,6,2048]{2,0,1:T(8,128)(2,1)}, u32[]{:S(2)}, u32[]{:S(2)}) collective-permute-start(bf16[20,6,2048]{2,0,1:T(8,128)(2,1)} %get-tuple-element.54), channel_id=1, source_target_pairs={{0,1},{1,2},{2,3},{3,4},{4,5},{5,6},{6,7},{8,9},{9,10},{10,11},{11... | collective-permute-start | bytes 1474568 | tf_op jit(solution)/shard_map/ppermute | solution.py:17
  45.6 47.2 %collective-permute-start.3 = (bf16[20,6,2048]{2,0,1:T(8,128)(2,1)}, bf16[20,6,2048]{2,0,1:T(8,128)(2,1)}, u32[]{:S(2)}, u32[]{:S(2)}) collective-permute-start(bf16[20,6,2048]{2,0,1:T(8,128)(2,1)} %get-tuple-element.55), channel_id=1, source_target_pairs={{1,0},{2,1},{3,2},{4,3},{5,4},{6,5},{7,6},{9,8},{10,9},{11,10},{12... | collective-permute-start | bytes 1474568 | tf_op jit(solution)/shard_map/ppermute | solution.py:20
  114.4 2.9 copy-start.9
  114.4 2.9 copy-start.11
  114.4 6.7 %slice-start = ((s8[4849664]{0:T(1024)(128)(4,1)}), s8[4194304]{0:T(1024)(128)(4,1)S(1)}, s32[]{:S(2)}) async-start(s8[4849664]{0:T(1024)(128)(4,1)} %bitcast.76), calls=%async_computation.1 | async-start | bytes 8388608
  117.3 3.8 %slice-start.1 = ((s8[4849664]{0:T(1024)(128)(4,1)}), s8[655360]{0:T(1024)(128)(4,1)S(1)}, s32[]{:S(2)}) async-start(s8[4849664]{0:T(1024)(128)(4,1)} %bitcast.76), calls=%async_computation.2 | async-start | bytes 1310720
  121.0 1.4 copy-start.14
  122.4 2.4 copy-start.5
  141.7 4.0 %copy-start.1 = (f32[20,28,2048]{2,1,0:T(8,128)S(1)}, f32[20,28,2048]{2,1,0:T(8,128)}, u32[]{:S(2)}) copy-start(f32[20,28,2048]{2,1,0:T(8,128)} %reshape.334) | copy-start | bytes 13762564
  147.7 6.8 %copy-start.12 = (bf16[16,128,64]{1,2,0:T(8,128)(2,1)S(1)}, bf16[16,128,64]{1,2,0:T(8,128)(2,1)}, u32[]{:S(2)}) copy-start(bf16[16,128,64]{1,2,0:T(8,128)(2,1)} %get-tuple-element.63) | copy-start | bytes 786436
  148.0 7.7 %copy-start.6 = (bf16[16,128,592]{1,2,0:T(8,128)(2,1)S(1)}, bf16[16,128,592]{1,2,0:T(8,128)(2,1)}, u32[]{:S(2)}) copy-start(bf16[16,128,592]{1,2,0:T(8,128)(2,1)} %copy-done.5) | copy-start | bytes 7274500
  149.4 7.7 %collective-permute-start.4 = (bf16[20,6,2048]{2,0,1:T(8,128)(2,1)S(1)}, bf16[20,6,2048]{2,0,1:T(8,128)(2,1)S(1)}, u32[]{:S(2)}, u32[]{:S(2)}) collective-permute-start(bf16[20,6,2048]{2,0,1:T(8,128)(2,1)S(1)} %copy.50), channel_id=1, source_target_pairs={{1,0},{2,1},{3,2},{4,3},{5,4},{6,5},{7,6},{9,8},{10,9},{11,10},{12... | collective-permute-start | bytes 1474568 | tf_op jit(solution)/shard_map/ppermute | solution.py:28
  150.7 13.0 %collective-permute-start.5 = (bf16[20,6,2048]{2,0,1:T(8,128)(2,1)}, bf16[20,6,2048]{2,0,1:T(8,128)(2,1)}, u32[]{:S(2)}, u32[]{:S(2)}) collective-permute-start(bf16[20,6,2048]{2,0,1:T(8,128)(2,1)} %copy.52), channel_id=1, source_target_pairs={{0,1},{1,2},{2,3},{3,4},{4,5},{5,6},{6,7},{8,9},{9,10},{10,11},{11... | collective-permute-start | bytes 1474568 | tf_op jit(solution)/shard_map/ppermute | solution.py:28
  172.5 4.3 %copy-start.3 = (f32[592,1024]{1,0:T(8,128)S(1)}, f32[592,1024]{1,0:T(8,128)}, u32[]{:S(2)}) copy-start(f32[592,1024]{1,0:T(8,128)} %copy.49) | copy-start | bytes 7274500
  172.5 4.3 %copy-start.4 = (f32[592,1024]{1,0:T(8,128)S(1)}, f32[592,1024]{1,0:T(8,128)}, u32[]{:S(2)}) copy-start(f32[592,1024]{1,0:T(8,128)} %copy.48) | copy-start | bytes 7274500
  175.4 2.2 copy-start.15
  175.4 11.4 %collective-permute-start.6 = (bf16[6,16,2048]{2,1,0:T(8,128)(2,1)}, bf16[6,16,2048]{2,1,0:T(8,128)(2,1)}, u32[]{:S(2)}, u32[]{:S(2)}) collective-permute-start(bf16[6,16,2048]{2,1,0:T(8,128)(2,1)} %get-tuple-element.57), channel_id=1, source_target_pairs={{8,0},{16,8},{24,16},{9,1},{17,9},{25,17},{10,2},{18,10},{26,18},{... | collective-permute-start | bytes 1179656 | tf_op jit(solution)/shard_map/ppermute | solution.py:28
  177.6 3.4 %copy-start.2 = (f32[20,16,2048]{2,1,0:T(8,128)S(1)}, f32[20,16,2048]{2,1,0:T(8,128)}, u32[]{:S(2)}) copy-start(f32[20,16,2048]{2,1,0:T(8,128)} %scatter-add.15) | copy-start | bytes 7864324
  181.1 11.6 %collective-permute-start.7 = (bf16[6,16,2048]{2,1,0:T(8,128)(2,1)S(1)}, bf16[6,16,2048]{2,1,0:T(8,128)(2,1)S(1)}, u32[]{:S(2)}, u32[]{:S(2)}) collective-permute-start(bf16[6,16,2048]{2,1,0:T(8,128)(2,1)S(1)} %get-tuple-element.56), channel_id=1, source_target_pairs={{0,8},{8,16},{16,24},{1,9},{9,17},{17,25},{2,10},{10,18},{18,26},{... | collective-permute-start | bytes 1179656 | tf_op jit(solution)/shard_map/ppermute | solution.py:28
  310.6 2.7 copy-start.7
Sparse Core Ops, SparseCore 0:
  177.7 131.7 all-reduce.3
where the time goes:
time: 323 us; the launch traced here: 322 us
  waiting for transfers between devices  137 us (42%)
  local copies, waits for them, and re-layouts  47.4 us (15%)
  blocking collectives  43.1 us (13%)
  matrix products  28.9 us (9%)
  other arithmetic  27 us (8%)
  starting transfers between devices  21.5 us (7%)
  between operations  17.1 us (5%)
    unnamed x2, waiting for transfers between devices  117 us
    all_gather x1, blocking collectives, shards(): global_kv = lax.all_gather(own_kv, ('rows', 'cols'), axis=0, tiled=True)  43.1 us
    scatter-add x2, local copies, waits for them, and re-layouts, shards(): centre.at[:, tile_cols - RAD:].add(from_right).at[:, :RAD].add(from_left)  13.2 us
    ppermute x2, waiting for transfers between devices, with_halo(): lax.ppermute(lax.slice_in_dim(block, 0, width, axis=dim), axis, backward)  13.2 us
    ppermute x4, starting transfers between devices, from_behind(): return lax.ppermute(x, axis, pairs)  11.1 us
    dot_general x5, matrix products, einsum_wide(): return jnp.einsum(form, left, right, preferred_element_type=jnp.float32)  8.87 us
    ppermute x2, starting transfers between devices, with_halo(): lax.ppermute(lax.slice_in_dim(block, block.shape[dim] - width, None, axis...  7.75 us
  transfers between devices with their start and end apart: 9, of which 5 were waited for; matrix products, arithmetic and copies ran while one was open for 7% of the time, Pallas kernels for 0%

commit v1 on v0

--- a/solution.py
+++ b/solution.py
@@ -7,6 +7,24 @@
 HEADS = 16
 KW = 13
 RAD = 6
+
+
+def in_order(parts, dim):
+    parts = jnp.moveaxis(parts, 0, dim)
+    shape = parts.shape
+    return parts.reshape(*shape[:dim], shape[dim] * shape[dim + 1], *shape[dim + 2 :])
+
+
+def doubled(x, axis):
+    size = lax.axis_size(axis)
+    tiles = x[None]
+    for level in range(size.bit_length() - 1):
+        bit = 1 << level
+        theirs = lax.ppermute(tiles, axis, [(i, i ^ bit) for i in range(size)])
+        both = jnp.stack([tiles, theirs])
+        upper = lax.axis_index(axis) >> level & 1
+        tiles = jnp.where(upper == 0, both, both[::-1]).reshape(-1, *x.shape)
+    return tiles
 
 
 def with_halo(block, sides, width):
@@ -78,7 +96,7 @@
         own_place % band_cols - first_col
     )
     own_kv = lax.dynamic_slice_in_dim(key_value, own_local, 1, 0)
-    global_kv = lax.all_gather(own_kv, ("rows", "cols"), axis=0, tiled=True)
+    global_kv = in_order(doubled(own_kv, ("rows", "cols")), 0)
     framed = with_halo(
         key_value.reshape(tile_rows, tile_cols, 2 * model_width), (("rows", 0), ("cols", 1)), RAD
     ).reshape(frame_rows * frame_cols, 2 * model_width)

time: 323 us -> 291 us (0.901)
  blocking collectives: 43.1 us -> 0 us
  starting transfers between devices: 21.5 us -> 35.8 us
  waiting for transfers between devices: 137 us -> 133 us
    all_gather x1 -> x0, blocking collectives: 43.1 us -> none  [shards(): global_kv = lax.all_gather(own_kv, ('rows', 'cols'), axis=0, tiled=True)]
    ppermute x2, waiting for transfers between devices: 13.2 us -> 3.67 us  [with_halo(): lax.ppermute(lax.slice_in_dim(block, 0, width, axis=dim), axis, backward)]
    ppermute x0 -> x5, starting transfers between devices: none -> 7.6 us  [doubled(): theirs = lax.ppermute(tiles, axis, [(i, i ^ bit) for i in range(size)])]
    ppermute x4, starting transfers between devices: 11.1 us -> 18.4 us  [from_behind(): return lax.ppermute(x, axis, pairs)]
    ppermute x0 -> x5, waiting for transfers between devices: none -> 6.83 us  [doubled(): theirs = lax.ppermute(tiles, axis, [(i, i ^ bit) for i in range(size)])]
  transfers between devices with their start and end apart: 9 -> 14, of which waited for: 5 -> 7; matrix products, arithmetic and copies ran while one was open for 7% -> 9% of each run, Pallas kernels for 0% -> 0%
where the time goes in v1:
time: 291 us; the launch traced here: 290 us
  waiting for transfers between devices  133 us (46%)
  local copies, waits for them, and re-layouts  48.7 us (17%)
  starting transfers between devices  35.8 us (12%)
  matrix products  29.8 us (10%)
  other arithmetic  25.8 us (9%)
  between operations  17.2 us (6%)
    unnamed x2, waiting for transfers between devices  117 us
    ppermute x4, starting transfers between devices, from_behind(): return lax.ppermute(x, axis, pairs)  18.4 us
    scatter-add x2, local copies, waits for them, and re-layouts, shards(): centre.at[:, tile_cols - RAD:].add(from_right).at[:, :RAD].add(from_left)  13.2 us
    dot_general x5, matrix products, einsum_wide(): return jnp.einsum(form, left, right, preferred_element_type=jnp.float32)  8.84 us
    ppermute x5, starting transfers between devices, doubled(): theirs = lax.ppermute(tiles, axis, [(i, i ^ bit) for i in range(size)])  7.6 us
    ppermute x2, starting transfers between devices, with_halo(): lax.ppermute(lax.slice_in_dim(block, block.shape[dim] - width, None, axis...  6.95 us
    ppermute x5, waiting for transfers between devices, doubled(): theirs = lax.ppermute(tiles, axis, [(i, i ^ bit) for i in range(size)])  6.83 us
    reshape x2, local copies, waits for them, and re-layouts, from_heads(): return x.transpose(1, 0, 2).reshape(count, heads * size)  6.35 us
  transfers between devices with their start and end apart: 14, of which 7 were waited for; matrix products, arithmetic and copies ran while one was open for 9% of the time, Pallas kernels for 0%

profile of v1, /device:TPU:0, one launch (start us, length us, event | category | flops | bytes accessed | tf_op | source)
XLA Modules:
  0.0 290.1 jit_solution(10839609557409828526)
XLA Ops:
  11.3 2.3 convolution_convert_fusion.4
  15.7 5.2 %collective-permute-start = (bf16[6,16,2048]{2,0,1:T(8,128)(2,1)}, bf16[6,16,2048]{2,0,1:T(8,128)(2,1)}, u32[]{:S(2)}, u32[]{:S(2)}) collective-permute-start(bf16[6,16,2048]{2,0,1:T(8,128)(2,1)} %copy.42), channel_id=1, source_target_pairs={{0,8},{8,16},{16,24},{1,9},{9,17},{17,25},{2,10},{10,18},{18,26},{... | collective-permute-start | bytes 1179656 | tf_op jit(solution)/shard_map/ppermute | solution.py:35
  23.3 2.7 convolution_convert_fusion.6
  29.6 2.1 collective-permute-done.5
  31.8 2.7 collective-permute-start.6
  36.6 2.7 collective-permute-start.7
  43.2 2.8 collective-permute-done.7
  51.2 3.7 %collective-permute-done.3 = bf16[20,6,2048]{2,0,1:T(8,128)(2,1)S(1)} collective-permute-done((bf16[20,6,2048]{2,0,1:T(8,128)(2,1)S(1)}, bf16[20,6,2048]{2,0,1:T(8,128)(2,1)S(1)}, u32[]{:S(2)}, u32[]{:S(2)}) %collective-permute-start.3) | collective-permute-done | bytes 491552 | tf_op jit(solution)/shard_map/ppermute | solution.py:38
  54.8 2.0 pad_maximum_fusion
  56.8 2.8 copy.45
  59.6 4.0 %reshape.336 = bf16[560,2048]{1,0:T(8,128)(2,1)} reshape(bf16[20,28,2048]{2,1,0:T(8,128)(2,1)} %copy.45) | data formatting | bytes 4587520 | tf_op jit(solution)/shard_map/reshape | solution.py:102
  63.6 3.2 %pad_maximum_fusion.1 = (bf16[592,1024]{1,0:T(8,128)(2,1)}, bf16[592,1024]{1,0:T(8,128)(2,1)}) fusion(bf16[32,2048]{1,0:T(8,128)(2,1)S(1)} %bitcast.110, bf16[560,2048]{1,0:T(8,128)(2,1)} %reshape.336), kind=kLoop, calls=%fused_computation.21 | loop fusion | flops 4849664 | bytes 4849664 | tf_op jit(solution)/shard_map/concatenate | solution.py:103
  68.6 2.4 copy.47
  71.0 5.0 %fusion.25 = (f32[16,128]{1,0:T(8,128)S(1)}, f32[16,128,592]{1,2,0:T(8,128)}) fusion(pred[128,592]{0,1:T(8,128)(4,1)S(1)} %concatenate.26.clone, bf16[16,128,64]{1,2,0:T(8,128)(2,1)} %bitcast.107, bf16[16,592,64]{1,2,0:T(8,128)(2,1)S(1)} %bitcast.92), kind=kOutput, calls=%fused_computation.81 | convolution fusion | flops 160039504 | bytes 6408192 | tf_op jit(solution)/shard_map/sub | solution.py:119
  76.0 2.9 %fusion.6 = bf16[16,128,592]{1,2,0:T(8,128)(2,1)S(1)} fusion(f32[16,128,592]{1,2,0:T(8,128)} %get-tuple-element.65, f32[16,128]{1,0:T(8,128)S(1)} %get-tuple-element.64), kind=kLoop, calls=%fused_computation.15 | loop fusion | flops 2424832 | bytes 7282688 | tf_op jit(solution)/shard_map/convert_element_type | solution.py:122
  80.3 2.4 fusion.28
  84.0 2.4 fusion.27
  86.5 3.2 %copy.50 = f32[592,1024]{1,0:T(8,128)} copy(f32[592,1024]{0,1:T(8,128)} %bitcast.88) | data formatting | bytes 4849664 | tf_op jit(solution)/shard_map/reshape | solution.py:67
  89.6 3.2 %copy.49 = f32[592,1024]{1,0:T(8,128)} copy(f32[592,1024]{0,1:T(8,128)} %bitcast.89) | data formatting | bytes 4849664 | tf_op jit(solution)/shard_map/reshape | solution.py:67
  92.8 5.0 %fusion.1 = f32[560,2048]{1,0:T(8,128)} fusion(f32[592,1024]{1,0:T(8,128)} %copy.49, f32[592,1024]{1,0:T(8,128)} %copy.50), kind=kLoop, calls=%fused_computation.6 | loop fusion | flops 1146880 | bytes 9437184 | tf_op jit(solution)/shard_map/concatenate | solution.py:140
  97.8 5.4 %reshape.350 = f32[20,28,2048]{2,1,0:T(8,128)} reshape(f32[560,2048]{1,0:T(8,128)} %fusion.1) | data formatting | bytes 9175040 | tf_op jit(solution)/shard_map/reshape | solution.py:143
  103.2 3.0 %convert.8 = bf16[20,28,2048]{2,1,0:T(8,128)(2,1)S(1)} convert(f32[20,28,2048]{2,1,0:T(8,128)} %reshape.350) | non-fusion elementwise | flops 1146880 | bytes 6881280 | tf_op jit(solution)/shard_map/convert.3
  107.3 2.0 slice.186
  112.2 11.2 %collective-permute-start.10 = (bf16[20,6,2048]{2,0,1:T(8,128)(2,1)}, bf16[20,6,2048]{2,0,1:T(8,128)(2,1)}, u32[]{:S(2)}, u32[]{:S(2)}) collective-permute-start(bf16[20,6,2048]{2,0,1:T(8,128)(2,1)} %copy.53), channel_id=1, source_target_pairs={{0,1},{1,2},{2,3},{3,4},{4,5},{5,6},{6,7},{8,9},{9,10},{10,11},{11... | collective-permute-start | bytes 1474568 | tf_op jit(solution)/shard_map/ppermute | solution.py:46
  126.3 6.2 %scatter-add.14 = f32[20,16,2048]{2,1,0:T(8,128)} dynamic-update-slice(f32[20,16,2048]{2,1,0:T(8,128)} %slice.186, f32[20,6,2048]{2,1,0:T(8,128)S(1)} %slice_add_fusion.1, s32[]{:T(128)} %constant.167.clone.1, s32[]{:T(128)} %constant.187.clone.1, s32[]{:T(128)} %constant.167.clone.1) | dynamic-update-slice | bytes 1966084 | tf_op jit(solution)/shard_map/scatter-add | solution.py:151
  134.3 7.0 %scatter-add.15 = f32[20,16,2048]{2,1,0:T(8,128)} dynamic-update-slice(f32[20,16,2048]{2,1,0:T(8,128)} %scatter-add.14, f32[20,6,2048]{2,1,0:T(8,128)S(1)} %slice_add_fusion, s32[]{:T(128)} %constant.167.clone.1, s32[]{:T(128)} %constant.167.clone.1, s32[]{:T(128)} %constant.167.clone.1) | dynamic-update-slice | bytes 1966084 | tf_op jit(solution)/shard_map/scatter-add | solution.py:151
  141.3 2.1 convert.9
  146.3 3.4 %fusion.26 = f32[128,1024]{1,0:T(8,128)} fusion(bf16[128,1024]{0,1:T(8,128)(2,1)S(1)} %bitcast.109, bf16[1024,1024]{1,0:T(8,128)(2,1)} %param.16), kind=kOutput, calls=%fused_computation.82 | convolution fusion | flops 268435456 | bytes 2883584 | tf_op jit(solution)/shard_map/dot_general | solution.py:162
  149.8 4.6 %collective-permute-start.12 = (bf16[6,16,2048]{2,1,0:T(8,128)(2,1)S(1)}, bf16[6,16,2048]{2,1,0:T(8,128)(2,1)S(1)}, u32[]{:S(2)}, u32[]{:S(2)}) collective-permute-start(bf16[6,16,2048]{2,1,0:T(8,128)(2,1)S(1)} %get-tuple-element.56), channel_id=1, source_target_pairs={{0,8},{8,16},{16,24},{1,9},{9,17},{17,25},{2,10},{10,18},{18,26},{... | collective-permute-start | bytes 1179656 | tf_op jit(solution)/shard_map/ppermute | solution.py:46
  156.2 4.9 %collective-permute-done.12 = bf16[6,16,2048]{2,1,0:T(8,128)(2,1)S(1)} collective-permute-done((bf16[6,16,2048]{2,1,0:T(8,128)(2,1)S(1)}, bf16[6,16,2048]{2,1,0:T(8,128)(2,1)S(1)}, u32[]{:S(2)}, u32[]{:S(2)}) %collective-permute-start.12) | collective-permute-done | bytes 393248 | tf_op jit(solution)/shard_map/ppermute | solution.py:46
  161.3 116.6 %all-reduce.4.cloned.1.call-done = f32[32,2048]{1,0:T(8,128)} async-done(((f32[32,2048]{1,0:T(8,128)}), f32[32,2048]{1,0:T(8,128)}) %all-reduce.4.cloned.1.call-update) | async-done | bytes 262160
  279.0 2.6 convolution_add_fusion.1
  (110 shorter events, 41.3 us)
Async XLA Ops:
  7.2 18.8 %copy-start = (bf16[1024,1024]{1,0:T(8,128)(2,1)S(1)}, bf16[1024,1024]{1,0:T(8,128)(2,1)}, u32[]{:S(2)}) copy-start(bf16[1024,1024]{1,0:T(8,128)(2,1)} %param.19) | copy-start | bytes 6291460
  7.2 6.4 %copy-start.10 = (bf16[8,16,1024]{2,1,0:T(8,128)(2,1)S(1)}, bf16[8,16,1024]{2,1,0:T(8,128)(2,1)}, u32[]{:S(2)}) copy-start(bf16[8,16,1024]{2,1,0:T(8,128)(2,1)} %param.15) | copy-start | bytes 786436
  7.2 270.7 %all-reduce.4.cloned.1.call-start = ((), (), s32[]{:S(2)}) async-start(), calls=%async_computation | async-start | bytes 524288
  11.3 2.3 copy-start.8
  14.1 13.8 %collective-permute-start.4 = (bf16[1,1,2048]{2,1,0:T(2,128)(2,1)S(1)}, bf16[1,1,2048]{2,1,0:T(2,128)(2,1)S(1)}, u32[]{:S(2)}, u32[]{:S(2)}) collective-permute-start(bf16[1,1,2048]{2,1,0:T(2,128)(2,1)S(1)} %bitcast.115), channel_id=1, source_target_pairs={{0,1},{1,0},{2,3},{3,2},{4,5},{5,4},{6,7},{7,6},{8,9},{9,8},{10,11... | collective-permute-start | bytes 12296 | tf_op jit(solution)/shard_map/ppermute | solution.py:23
  15.7 30.4 %collective-permute-start = (bf16[6,16,2048]{2,0,1:T(8,128)(2,1)}, bf16[6,16,2048]{2,0,1:T(8,128)(2,1)}, u32[]{:S(2)}, u32[]{:S(2)}) collective-permute-start(bf16[6,16,2048]{2,0,1:T(8,128)(2,1)} %copy.42), channel_id=1, source_target_pairs={{0,8},{8,16},{16,24},{1,9},{9,17},{17,25},{2,10},{10,18},{18,26},{... | collective-permute-start | bytes 1179656 | tf_op jit(solution)/shard_map/ppermute | solution.py:35
  21.9 24.2 %collective-permute-start.1 = (bf16[6,16,2048]{2,0,1:T(8,128)(2,1)}, bf16[6,16,2048]{2,0,1:T(8,128)(2,1)}, u32[]{:S(2)}, u32[]{:S(2)}) collective-permute-start(bf16[6,16,2048]{2,0,1:T(8,128)(2,1)} %copy.43), channel_id=1, source_target_pairs={{8,0},{16,8},{24,16},{9,1},{17,9},{25,17},{10,2},{18,10},{26,18},{... | collective-permute-start | bytes 1179656 | tf_op jit(solution)/shard_map/ppermute | solution.py:38
  28.0 3.7 %collective-permute-start.5 = (bf16[2,1,2048]{2,0,1:T(2,128)(2,1)S(1)}, bf16[2,1,2048]{2,0,1:T(2,128)(2,1)S(1)}, u32[]{:S(2)}, u32[]{:S(2)}) collective-permute-start(bf16[2,1,2048]{2,0,1:T(2,128)(2,1)S(1)} %bitcast.117), channel_id=1, source_target_pairs={{0,2},{1,3},{2,0},{3,1},{4,6},{5,7},{6,4},{7,5},{8,10},{9,11},{10,... | collective-permute-start | bytes 24584 | tf_op jit(solution)/shard_map/ppermute | solution.py:23
  31.8 4.7 %collective-permute-start.6 = (bf16[4,1,2048]{2,0,1:T(4,128)(2,1)S(1)}, bf16[4,1,2048]{2,0,1:T(4,128)(2,1)S(1)}, u32[]{:S(2)}, u32[]{:S(2)}) collective-permute-start(bf16[4,1,2048]{2,0,1:T(4,128)(2,1)S(1)} %reshape.338), channel_id=1, source_target_pairs={{0,4},{1,5},{2,6},{3,7},{4,0},{5,1},{6,2},{7,3},{8,12},{9,13},{10,... | collective-permute-start | bytes 49160 | tf_op jit(solution)/shard_map/ppermute | solution.py:23
  36.6 9.4 %collective-permute-start.7 = (bf16[8,1,2048]{2,0,1:T(8,128)(2,1)S(1)}, bf16[8,1,2048]{2,0,1:T(8,128)(2,1)S(1)}, u32[]{:S(2)}, u32[]{:S(2)}) collective-permute-start(bf16[8,1,2048]{2,0,1:T(8,128)(2,1)S(1)} %reshape.339), channel_id=1, source_target_pairs={{0,8},{1,9},{2,10},{3,11},{4,12},{5,13},{6,14},{7,15},{8,0},{9,1},... | collective-permute-start | bytes 98312 | tf_op jit(solution)/shard_map/ppermute | solution.py:23
  46.0 5.0 %collective-permute-start.8 = (bf16[16,1,2048]{2,0,1:T(8,128)(2,1)S(1)}, bf16[16,1,2048]{2,0,1:T(8,128)(2,1)S(1)}, u32[]{:S(2)}, u32[]{:S(2)}) collective-permute-start(bf16[16,1,2048]{2,0,1:T(8,128)(2,1)S(1)} %get-tuple-element.61), channel_id=1, source_target_pairs={{0,16},{1,17},{2,18},{3,19},{4,20},{5,21},{6,22},{7,23},{8,24},{9,... | collective-permute-start | bytes 196616 | tf_op jit(solution)/shard_map/ppermute | solution.py:23
  47.8 3.3 %collective-permute-start.2 = (bf16[20,6,2048]{2,0,1:T(8,128)(2,1)S(1)}, bf16[20,6,2048]{2,0,1:T(8,128)(2,1)S(1)}, u32[]{:S(2)}, u32[]{:S(2)}) collective-permute-start(bf16[20,6,2048]{2,0,1:T(8,128)(2,1)S(1)} %get-tuple-element.54), channel_id=1, source_target_pairs={{0,1},{1,2},{2,3},{3,4},{4,5},{5,6},{6,7},{8,9},{9,10},{10,11},{11... | collective-permute-start | bytes 1474568 | tf_op jit(solution)/shard_map/ppermute | solution.py:35
  49.6 5.2 %collective-permute-start.3 = (bf16[20,6,2048]{2,0,1:T(8,128)(2,1)S(1)}, bf16[20,6,2048]{2,0,1:T(8,128)(2,1)S(1)}, u32[]{:S(2)}, u32[]{:S(2)}) collective-permute-start(bf16[20,6,2048]{2,0,1:T(8,128)(2,1)S(1)} %get-tuple-element.55), channel_id=1, source_target_pairs={{1,0},{2,1},{3,2},{4,3},{5,4},{6,5},{7,6},{9,8},{10,9},{11,10},{12... | collective-permute-start | bytes 1474568 | tf_op jit(solution)/shard_map/ppermute | solution.py:38
  76.0 2.9 %copy-start.9 = (bf16[592,1024]{0,1:T(8,128)(2,1)S(1)}, bf16[592,1024]{0,1:T(8,128)(2,1)}, u32[]{:S(2)}) copy-start(bf16[592,1024]{0,1:T(8,128)(2,1)} %copy.47) | copy-start | bytes 3637252
  76.0 2.9 %copy-start.11 = (bf16[128,1024]{0,1:T(8,128)(2,1)S(1)}, bf16[128,1024]{0,1:T(8,128)(2,1)}, u32[]{:S(2)}) copy-start(bf16[128,1024]{0,1:T(8,128)(2,1)} %copy.48) | copy-start | bytes 786436
  76.0 6.7 %slice-start = ((s8[4849664]{0:T(1024)(128)(4,1)}), s8[4194304]{0:T(1024)(128)(4,1)S(1)}, s32[]{:S(2)}) async-start(s8[4849664]{0:T(1024)(128)(4,1)} %bitcast.96), calls=%async_computation.1 | async-start | bytes 8388608
  78.9 3.7 %slice-start.1 = ((s8[4849664]{0:T(1024)(128)(4,1)}), s8[655360]{0:T(1024)(128)(4,1)S(1)}, s32[]{:S(2)}) async-start(s8[4849664]{0:T(1024)(128)(4,1)} %bitcast.96), calls=%async_computation.2 | async-start | bytes 1310720
  82.7 1.4 copy-start.13
  84.0 2.4 copy-start.5
  103.2 4.0 %copy-start.1 = (f32[20,28,2048]{2,1,0:T(8,128)S(1)}, f32[20,28,2048]{2,1,0:T(8,128)}, u32[]{:S(2)}) copy-start(f32[20,28,2048]{2,1,0:T(8,128)} %reshape.350) | copy-start | bytes 13762564
  109.2 14.1 %copy-start.12 = (bf16[16,128,64]{1,2,0:T(8,128)(2,1)S(1)}, bf16[16,128,64]{1,2,0:T(8,128)(2,1)}, u32[]{:S(2)}) copy-start(bf16[16,128,64]{1,2,0:T(8,128)(2,1)} %get-tuple-element.67) | copy-start | bytes 786436
  109.5 15.1 %copy-start.6 = (bf16[16,128,592]{1,2,0:T(8,128)(2,1)S(1)}, bf16[16,128,592]{1,2,0:T(8,128)(2,1)}, u32[]{:S(2)}) copy-start(bf16[16,128,592]{1,2,0:T(8,128)(2,1)} %copy-done.5) | copy-start | bytes 7274500
  110.9 15.0 %collective-permute-start.9 = (bf16[20,6,2048]{2,0,1:T(8,128)(2,1)S(1)}, bf16[20,6,2048]{2,0,1:T(8,128)(2,1)S(1)}, u32[]{:S(2)}, u32[]{:S(2)}) collective-permute-start(bf16[20,6,2048]{2,0,1:T(8,128)(2,1)S(1)} %copy.51), channel_id=1, source_target_pairs={{1,0},{2,1},{3,2},{4,3},{5,4},{6,5},{7,6},{9,8},{10,9},{11,10},{12... | collective-permute-start | bytes 1474568 | tf_op jit(solution)/shard_map/ppermute | solution.py:46
  112.2 20.3 %collective-permute-start.10 = (bf16[20,6,2048]{2,0,1:T(8,128)(2,1)}, bf16[20,6,2048]{2,0,1:T(8,128)(2,1)}, u32[]{:S(2)}, u32[]{:S(2)}) collective-permute-start(bf16[20,6,2048]{2,0,1:T(8,128)(2,1)} %copy.53), channel_id=1, source_target_pairs={{0,1},{1,2},{2,3},{3,4},{4,5},{5,6},{6,7},{8,9},{9,10},{10,11},{11... | collective-permute-start | bytes 1474568 | tf_op jit(solution)/shard_map/ppermute | solution.py:46
  141.3 4.3 %copy-start.3 = (f32[592,1024]{1,0:T(8,128)S(1)}, f32[592,1024]{1,0:T(8,128)}, u32[]{:S(2)}) copy-start(f32[592,1024]{1,0:T(8,128)} %copy.50) | copy-start | bytes 7274500
  141.3 4.3 %copy-start.4 = (f32[592,1024]{1,0:T(8,128)S(1)}, f32[592,1024]{1,0:T(8,128)}, u32[]{:S(2)}) copy-start(f32[592,1024]{1,0:T(8,128)} %copy.49) | copy-start | bytes 7274500
  144.1 2.2 copy-start.14
  144.1 10.9 %collective-permute-start.11 = (bf16[6,16,2048]{2,1,0:T(8,128)(2,1)}, bf16[6,16,2048]{2,1,0:T(8,128)(2,1)}, u32[]{:S(2)}, u32[]{:S(2)}) collective-permute-start(bf16[6,16,2048]{2,1,0:T(8,128)(2,1)} %get-tuple-element.57), channel_id=1, source_target_pairs={{8,0},{16,8},{24,16},{9,1},{17,9},{25,17},{10,2},{18,10},{26,18},{... | collective-permute-start | bytes 1179656 | tf_op jit(solution)/shard_map/ppermute | solution.py:46
  146.3 3.4 %copy-start.2 = (f32[20,16,2048]{2,1,0:T(8,128)S(1)}, f32[20,16,2048]{2,1,0:T(8,128)}, u32[]{:S(2)}) copy-start(f32[20,16,2048]{2,1,0:T(8,128)} %scatter-add.15) | copy-start | bytes 7864324
  149.8 11.3 %collective-permute-start.12 = (bf16[6,16,2048]{2,1,0:T(8,128)(2,1)S(1)}, bf16[6,16,2048]{2,1,0:T(8,128)(2,1)S(1)}, u32[]{:S(2)}, u32[]{:S(2)}) collective-permute-start(bf16[6,16,2048]{2,1,0:T(8,128)(2,1)S(1)} %get-tuple-element.56), channel_id=1, source_target_pairs={{0,8},{8,16},{16,24},{1,9},{9,17},{17,25},{2,10},{10,18},{18,26},{... | collective-permute-start | bytes 1179656 | tf_op jit(solution)/shard_map/ppermute | solution.py:46
  279.0 2.7 copy-start.7
Sparse Core Ops, SparseCore 0:
  146.4 131.3 all-reduce.3
